TPU v7x, 128 devices: a whole 4x4x4 slice. The times are simulated.
128 devices in a mesh: seq: 4 (over x_hi, core), tensor: 32 (over y, x_lo, z).
Axes of the slice: x: 4 (x_hi: 2, x_lo: 2; x = x_hi * 2 + x_lo), y: 4, z: 4, core: 2. Of those that a mesh axis runs over, the one named last changes fastest.
Arguments:
- hidden_in: bfloat16 [8192, 4608], P(('seq', 'tensor'))
- norm_gain: float32 [4608], replicated, may hold values from 0.5 to 1.5
- query_weight: bfloat16 [4608, 4096], P(None, 'tensor')
- key_weight: bfloat16 [4608, 2048], P(None, 'tensor'), may hold values from -0.09375 to 0.09375
- value_weight: bfloat16 [4608, 2048], P(None, 'tensor'), may hold values from -0.09375 to 0.09375
- out_weight: bfloat16 [4096, 4608], P('tensor'), may hold values from -0.09375 to 0.09375
- post_gain: float32 [4608], replicated, may hold values from 0.5 to 1.5
- seg_lengths: int32 [3], replicated, may hold values from 256 to 4096, as said below
- segment_ids: int32 [8192], replicated, may hold values from 0 to 2, as said below
- slot_map: int32 [3], replicated, may hold values from 0 to 2, each once
Outputs:
- hidden_out: bfloat16 [8192, 4608], P(('seq', 'tensor'))
- key_cache: bfloat16 [3, 4096, 2048], P(None, 'seq', 'tensor')
- value_cache: bfloat16 [3, 4096, 2048], P(None, 'seq', 'tensor')
Inputs may be any that keep to these rules, and one draw needn't show every extreme that they name: `seg_lengths`: the 3 lengths sum to 8192; the second request is the longest, with exactly 4096 tokens. `segment_ids`: requests follow one another in order: request r holds seg_lengths[r] consecutive tokens, starting where request r - 1 ends. `slot_map`: each cache slot is named by exactly one request.
All inputs are finite; a program needn't handle non-finite values.
Results may differ from a plain program's by a relative error of at most 0.02.
Values may be sent and summed in bfloat16 or wider, within the bound.
No kernel may reach another device: no remote copies, remote signals or barrier semaphores. Data moves between devices by JAX's collectives and lax.ppermute only.
A program may use at most 128 MiB of HBM per device.

v0:
```python
import math

import jax
import jax.numpy as jnp
from jax import lax
from jax.sharding import PartitionSpec as P

HD = 128


EPSILON = 1e-06
SOFTCAP = 50.0
QUERY_SCALE = 144.0 ** (-0.5)
SCORE_SHIFT = 20.0
ROPE_BASE = 10000.0


def partner(value, axis, distance):
    mask = 2**distance
    pairs = [(source, source ^ mask) for source in range(lax.axis_size(axis))]
    return lax.ppermute(value, axis, pairs)


def rms_scale(values, gain):
    mean_sq = jnp.mean(values * values, axis=-1, keepdims=True)
    return values * lax.rsqrt(mean_sq + EPSILON) * gain


def rotate(values, positions):
    head_dim = values.shape[-1]
    half_dim = head_dim // 2
    freqs = ROPE_BASE ** (-2.0 * jnp.arange(half_dim, dtype=jnp.float32) / head_dim)
    angles = positions.astype(jnp.float32)[:, None] * freqs[None, :]
    cosine = jnp.cos(angles)[:, None, :]
    sine = jnp.sin(angles)[:, None, :]
    first = values[..., :half_dim]
    second = values[..., half_dim:]
    return jnp.concatenate(
        [first * cosine - second * sine, second * cosine + first * sine], axis=-1
    )


def token_positions(row_ids, row_segments, seg_lengths):
    starts = jnp.cumsum(seg_lengths) - seg_lengths
    request_ids = jnp.arange(seg_lengths.shape[0], dtype=jnp.int32)
    picked = jnp.sum(
        jnp.where(row_segments[:, None] == request_ids[None, :], starts[None, :], 0), axis=1
    )
    return row_ids - picked


def on_device(
    hidden_in,
    norm_gain,
    query_weight,
    key_weight,
    value_weight,
    out_weight,
    post_gain,
    seg_lengths,
    segment_ids,
    slot_map,
):
    n_tensor = lax.axis_size("tensor")
    n_seq = lax.axis_size("seq")
    local_rows = hidden_in.shape[0]
    shard_rows = local_rows * n_tensor
    half_rows = shard_rows // 2
    head_dim = HD
    q_cols = query_weight.shape[1]
    kv_cols = key_weight.shape[1]
    q_heads = q_cols // head_dim
    tensor_index = lax.axis_index("tensor")
    seq_index = lax.axis_index("seq")
    slot_count = seg_lengths.shape[0]
    hidden = hidden_in.astype(jnp.float32)
    normed = rms_scale(hidden, norm_gain).astype(jnp.bfloat16)
    joined = jnp.concatenate([query_weight, key_weight, value_weight], axis=1)
    mixed = jnp.dot(
        lax.all_gather(normed, "tensor", axis=0, tiled=True),
        joined,
        preferred_element_type=jnp.float32,
    )
    queries = mixed[:, :q_cols]
    own_key = mixed[:, q_cols : q_cols + kv_cols]
    own_value = mixed[:, q_cols + kv_cols :]
    other_key, other_value = (
        partner(own_key.astype(jnp.bfloat16), "tensor", 0).astype(own_key.dtype),
        partner(own_value.astype(jnp.bfloat16), "tensor", 0).astype(own_value.dtype),
    )
    leading = tensor_index % 2 == 0
    full_key = jnp.where(
        leading, jnp.concatenate([own_key, other_key], 1), jnp.concatenate([other_key, own_key], 1)
    )
    full_value = jnp.where(
        leading,
        jnp.concatenate([own_value, other_value], 1),
        jnp.concatenate([other_value, own_value], 1),
    )
    kv_heads = 1
    own_offset = tensor_index % 2 * kv_cols
    group = q_heads // kv_heads
    shard_start = seq_index * shard_rows
    row_ids = shard_start + jnp.arange(shard_rows, dtype=jnp.int32)
    shard_segments = lax.dynamic_slice_in_dim(segment_ids, shard_start, shard_rows, 0)
    positions = token_positions(row_ids, shard_segments, seg_lengths)
    q_rot = rotate(queries.reshape(shard_rows, q_heads, head_dim), positions).astype(jnp.bfloat16)
    k_rot = rotate(full_key.reshape(shard_rows, kv_heads, head_dim), positions).astype(jnp.bfloat16)
    v_rot = full_value.reshape(shard_rows, kv_heads, head_dim).astype(jnp.bfloat16)
    q_flat = q_rot.reshape(2, half_rows, q_cols)
    my_queries = q_flat
    q_starts = shard_start + jnp.arange(2, dtype=jnp.int32) * half_rows
    my_queries = my_queries.reshape(2, half_rows, kv_heads, group, head_dim)
    q_rows = [
        q_starts[which_half] + jnp.arange(half_rows, dtype=jnp.int32) for which_half in range(2)
    ]
    q_segs = [
        lax.dynamic_slice_in_dim(segment_ids, q_starts[which_half], half_rows, 0)
        for which_half in range(2)
    ]
    zero_numer = jnp.zeros((half_rows, kv_heads, group, head_dim), jnp.float32)
    zero_denom = jnp.zeros((kv_heads, group, half_rows), jnp.float32)
    start_state = ((zero_numer, zero_numer), (zero_denom, zero_denom))
    cache_len = shard_rows * n_seq // 2
    part_len = cache_len // n_seq
    request_ids = jnp.arange(slot_count, dtype=jnp.int32)
    starts = jnp.cumsum(seg_lengths) - seg_lengths
    slot_requests = [
        jnp.sum(jnp.where(slot_map == slot_index, request_ids, 0))
        for slot_index in range(slot_count)
    ]
    slot_starts = [
        jnp.sum(jnp.where(request_ids == slot_requests[slot_index], starts, 0))
        for slot_index in range(slot_count)
    ]
    key_rows = lax.all_gather(k_rot, "seq", axis=0, tiled=True)
    value_rows = lax.all_gather(v_rot, "seq", axis=0, tiled=True)
    row_count = key_rows.shape[0]
    width = math.gcd(512, row_count)

    def tile(tile_index, state):
        numer, denom = state
        k_start = tile_index * width
        k_block = lax.dynamic_slice_in_dim(key_rows, tile_index * width, width, 0)
        v_block = lax.dynamic_slice_in_dim(value_rows, tile_index * width, width, 0)
        k_segs = lax.dynamic_slice_in_dim(segment_ids, k_start, width, 0)
        k_rows = k_start + jnp.arange(width, dtype=jnp.int32)
        new_numer = []
        new_denom = []
        for which_half in range(2):

            def compute(pair, which_half=which_half):
                numer_one, denom_one = pair
                scores = (
                    jnp.einsum(
                        "qcgd,kcd->cgqk",
                        my_queries[which_half],
                        k_block,
                        preferred_element_type=jnp.float32,
                    )
                    * QUERY_SCALE
                )
                scores = SOFTCAP * jnp.tanh(scores / SOFTCAP)
                live = (k_rows[None, :] <= q_rows[which_half][:, None]) & (
                    k_segs[None, :] == q_segs[which_half][:, None]
                )
                weights = jnp.where(live[None, None], jnp.exp(scores - SCORE_SHIFT), 0.0)
                denom_one = denom_one + jnp.sum(weights, axis=-1)
                numer_one = numer_one + jnp.einsum(
                    "cgqk,kcd->qcgd",
                    weights.astype(jnp.bfloat16),
                    v_block,
                    preferred_element_type=jnp.float32,
                )
                return (numer_one, denom_one)

            useful = (
                (k_start <= q_starts[which_half] + half_rows - 1)
                & (k_segs[0] <= q_segs[which_half][-1])
                & (k_segs[-1] >= q_segs[which_half][0])
            )
            numer_one, denom_one = lax.cond(
                useful, compute, lambda pair: pair, (numer[which_half], denom[which_half])
            )
            new_numer.append(numer_one)
            new_denom.append(denom_one)
        return (tuple(new_numer), tuple(new_denom))

    numer, denom = lax.fori_loop(0, row_count // width, tile, start_state)
    own_keys = lax.dynamic_slice_in_dim(
        k_rot.reshape(shard_rows, kv_heads * head_dim), own_offset, kv_cols, 1
    )
    own_values = lax.dynamic_slice_in_dim(
        v_rot.reshape(shard_rows, kv_heads * head_dim), own_offset, kv_cols, 1
    )
    seg_local = jnp.pad(shard_segments, (part_len, part_len), constant_values=-1)
    keys_local = jnp.pad(own_keys, ((part_len, part_len), (0, 0)))
    values_local = jnp.pad(own_values, ((part_len, part_len), (0, 0)))
    send_key_list = []
    send_value_list = []
    for target in range(n_seq):
        key_row = []
        value_row = []
        for slot_index in range(slot_count):
            offset = slot_starts[slot_index] + target * part_len - shard_start
            window = jnp.clip(offset, -part_len, shard_rows) + part_len
            keep = (
                lax.dynamic_slice_in_dim(seg_local, window, part_len, 0)
                == slot_requests[slot_index]
            )[:, None]
            key_row.append(
                jnp.where(
                    keep,
                    lax.dynamic_slice_in_dim(keys_local, window, part_len, 0),
                    jnp.zeros((), jnp.bfloat16),
                )
            )
            value_row.append(
                jnp.where(
                    keep,
                    lax.dynamic_slice_in_dim(values_local, window, part_len, 0),
                    jnp.zeros((), jnp.bfloat16),
                )
            )
        send_key_list.append(jnp.stack(key_row))
        send_value_list.append(jnp.stack(value_row))
    send_keys = jnp.stack(send_key_list)
    send_values = jnp.stack(send_value_list)
    recv_keys, recv_values = (
        lax.all_to_all(send_keys, "seq", split_axis=0, concat_axis=0, tiled=True),
        lax.all_to_all(send_values, "seq", split_axis=0, concat_axis=0, tiled=True),
    )
    cache_keys = recv_keys[0]
    cache_values = recv_values[0]
    for source in range(1, n_seq):
        cache_keys = cache_keys + recv_keys[source]
        cache_values = cache_values + recv_values[source]
    finished = []
    for which_half in range(2):
        denom_rows = jnp.transpose(denom[which_half], (2, 0, 1))[..., None]
        finished.append(
            (numer[which_half] / denom_rows).astype(jnp.bfloat16).reshape(half_rows, q_cols)
        )
    attended = jnp.stack(finished)
    attn_rows = attended.reshape(shard_rows, q_cols)
    projected = lax.psum_scatter(
        jnp.dot(attn_rows, out_weight, preferred_element_type=jnp.float32).astype(jnp.bfloat16),
        "tensor",
        scatter_dimension=0,
        tiled=True,
    ).astype(jnp.float32)
    hidden_out = (hidden + rms_scale(projected, post_gain)).astype(jnp.bfloat16)
    return (hidden_out, cache_keys, cache_values)


def solution(mesh):
    return jax.shard_map(
        on_device,
        mesh=mesh,
        in_specs=(
            P(("seq", "tensor"), None),
            P(),
            P(None, "tensor"),
            P(None, "tensor"),
            P(None, "tensor"),
            P("tensor", None),
            P(),
            P(),
            P(),
            P(),
        ),
        out_specs=(P(("seq", "tensor"), None), P(None, "seq", "tensor"), P(None, "seq", "tensor")),
        check_vma=False,
    )
```

profile of v0, /device:TPU:4, one launch (start us, length us, event | category | flops | bytes accessed | tf_op | source)
XLA Modules:
  0.0 749.3 jit_solution(10679060349301609649)
XLA Ops:
  18.7 206.8 %all-gather.4.cloned.1.call-done = bf16[2048,4608]{1,0:T(8,128)(2,1)} async-done(((bf16[64,4608]{1,0:T(8,128)(2,1)}), bf16[2048,4608]{1,0:T(8,128)(2,1)}) %all-gather.4.cloned.1.call-update) | async-done | bytes 18874384 | tf_op jit(solution)/shard_map/all_gather | solution.py:80
  225.5 10.9 %fusion.18 = f32[2048,256]{0,1:T(8,128)S(1)} fusion(bf16[2048,4608]{1,0:T(8,128)(2,1)} %all-gather.4.cloned.1.call-done, bf16[4608,64]{1,0:T(8,128)(2,1)S(1)} %copy.26, bf16[4608,64]{1,0:T(8,128)(2,1)S(1)} %copy.25, bf16[4608,128]{1,0:T(8,128)(2,1)} %param.18), kind=kOutput, calls=%fused_computation.26 | convolution fusion | flops 4838916096 | bytes 23330816 | tf_op jit(solution)/shard_map/dot_general | solution.py:79
  236.7 7.8 %collective-permute-done = bf16[2048,64]{0,1:T(8,128)(2,1)S(1)} collective-permute-done((bf16[2048,64]{0,1:T(8,128)(2,1)S(1)}, bf16[2048,64]{0,1:T(8,128)(2,1)S(1)}, u32[]{:S(2)}, u32[]{:S(2)}) %collective-permute-start) | collective-permute-done | bytes 262176 | tf_op jit(solution)/shard_map/ppermute | solution.py:21
  248.4 6.7 collective-permute-done.1
  264.5 4.7 all-gather.6.cloned.1.call-done
  269.1 27.7 %all-gather.8.cloned.1.call-done = bf16[8192,1,128]{0,2,1:T(8,128)(2,1)} async-done(((bf16[2048,1,128]{0,2,1:T(8,128)(2,1)}), bf16[8192,1,128]{0,2,1:T(8,128)(2,1)}) %all-gather.8.cloned.1.call-update) | async-done | bytes 2097168 | tf_op jit(solution)/shard_map/all_gather | solution.py:137
  297.0 181.7 %while.23 = (s32[]{:T(128)}, f32[1024,1,1,128]{3,0,2,1:T(8,128)S(1)}, f32[1024,1,1,128]{3,0,2,1:T(8,128)S(1)}, f32[1,1,1024]{2,1,0:T(1,128)S(1)}, f32[1,1,1024]{...) while((s32[]{:T(128)}, ...), condition=%wide.region_10.11_spmd.clone, body=%wide.region_3.10_spmd.clone.sunk | while | flops 546572800 | bytes 8477275 | solution.py:189
  327.4 3.1 conditional.7
  341.9 3.2 conditional.7
  347.5 3.1 conditional.6
  356.3 3.1 conditional.7
  370.8 3.2 conditional.7
  376.4 3.1 conditional.6
  385.3 3.1 conditional.7
  399.8 3.2 conditional.7
  414.2 3.1 conditional.7
  428.7 3.2 conditional.7
  440.1 3.2 conditional.7
  479.1 9.1 %convolution_convert_fusion = bf16[2048,4608]{1,0:T(8,128)(2,1)} fusion(bf16[2048,128]{1,0:T(8,128)(2,1)S(1)} %bitcast.173, bf16[128,4608]{1,0:T(8,128)(2,1)S(1)} %copy-done), kind=kOutput, calls=%fused_computation.25 | convolution fusion | flops 2425356288 | bytes 20578304 | tf_op jit(solution)/shard_map/dot_general | solution.py:247
  501.8 4.8 all-to-all-start.1
  509.3 32.0 %all-to-all-done.1 = bf16[4,3,1024,64]{2,3,1,0:T(8,128)(2,1)S(1)} async-done(((bf16[4,3,1024,64]{2,3,1,0:T(8,128)(2,1)}), bf16[4,3,1024,64]{2,3,1,0:T(8,128)(2,1)S(1)}, u32[]{:S(2)}, u32[]{:S(2)}) %all-to-all-start.1) | async-done | bytes 1572896 | tf_op jit(solution)/shard_map/all_to_all | solution.py:231
  541.3 8.0 %all-to-all-start = ((bf16[4,3,1024,64]{2,3,1,0:T(8,128)(2,1)}), bf16[4,3,1024,64]{2,3,1,0:T(8,128)(2,1)}, u32[]{:S(2)}, u32[]{:S(2)}) async-start(bf16[4,3,1024,64]{2,3,1,0:T(8,128)(2,1)} %pad_maximum_fusion), calls=%async_computation.1 | async-start | bytes 3145728 | tf_op jit(solution)/shard_map/all_to_all | solution.py:230
  550.1 34.4 %all-to-all-done = bf16[4,3,1024,64]{2,3,1,0:T(8,128)(2,1)} async-done(((bf16[4,3,1024,64]{2,3,1,0:T(8,128)(2,1)}), bf16[4,3,1024,64]{2,3,1,0:T(8,128)(2,1)}, u32[]{:S(2)}, u32[]{:S(2)}) %all-to-all-start) | async-done | bytes 1572896 | tf_op jit(solution)/shard_map/all_to_all | solution.py:230
  586.7 152.6 %reduce-scatter.2.cloned.1.call-done = bf16[64,4608]{1,0:T(8,128)(2,1)} async-done(((bf16[2048,4608]{1,0:T(8,128)(2,1)}), bf16[64,4608]{1,0:T(8,128)(2,1)}) %reduce-scatter.2.cloned.1.call-update) | async-done | bytes 589840 | tf_op jit(solution)/shard_map/reduce_scatter | solution.py:246
  (304 shorter events, 152.4 us)
Async XLA Ops:
  7.2 471.9 %copy-start = (bf16[128,4608]{1,0:T(8,128)(2,1)S(1)}, bf16[128,4608]{1,0:T(8,128)(2,1)}, u32[]{:S(2)}) copy-start(bf16[128,4608]{1,0:T(8,128)(2,1)} %param.21) | copy-start | bytes 3538948
  7.2 3.7 copy-start.3
  7.2 218.3 %all-gather.4.cloned.1.call-start = ((), (), s32[]{:S(2)}) async-start(), calls=%async_computation.3 | async-start | bytes 19464192 | tf_op jit(solution)/shard_map/all_gather | solution.py:80
  10.8 2.5 copy-start.5
  10.8 258.3 %all-gather.6.cloned.1.call-start = ((), (), s32[]{:S(2)}) async-start(), calls=%async_computation.4 | async-start | bytes 2621440 | tf_op jit(solution)/shard_map/all_gather | solution.py:136
  236.5 8.1 %copy-start.6 = (f32[64]{0:T(128)S(1)}, f32[64]{0:T(128)}, u32[]{:S(2)}) copy-start(f32[64]{0:T(128)} %multiply_power_fusion) | copy-start | bytes 772
  236.6 8.0 %collective-permute-start = (bf16[2048,64]{0,1:T(8,128)(2,1)S(1)}, bf16[2048,64]{0,1:T(8,128)(2,1)S(1)}, u32[]{:S(2)}, u32[]{:S(2)}) collective-permute-start(bf16[2048,64]{0,1:T(8,128)(2,1)S(1)} %get-tuple-element.605), channel_id=1, source_target_pairs={{0,1},{1,0},{2,3},{3,2},{4,5},{5,4},{6,7},{7,6},{8,9},{9,8},{10,11... | collective-permute-start | bytes 786440 | tf_op jit(solution)/shard_map/ppermute | solution.py:21
  248.0 48.9 %all-gather.8.cloned.1.call-start = ((), (), s32[]{:S(2)}) async-start(), calls=%async_computation.5 | async-start | bytes 2621440 | tf_op jit(solution)/shard_map/all_gather | solution.py:137
  248.0 7.1 collective-permute-start.1
  256.1 483.2 %reduce-scatter.2.cloned.1.call-start = ((), (), s32[]{:S(2)}) async-start(), calls=%async_computation.6 | async-start | bytes 19464192 | tf_op jit(solution)/shard_map/reduce_scatter | solution.py:246
  488.2 11.1 %copy-start.2 = (bf16[2048,1,128]{0,2,1:T(8,128)(2,1)S(1)}, bf16[2048,1,128]{0,2,1:T(8,128)(2,1)}, u32[]{:S(2)}) copy-start(bf16[2048,1,128]{0,2,1:T(8,128)(2,1)} %fusion.30) | copy-start | bytes 1572868
  501.8 39.5 %all-to-all-start.1 = ((bf16[4,3,1024,64]{2,3,1,0:T(8,128)(2,1)}), bf16[4,3,1024,64]{2,3,1,0:T(8,128)(2,1)S(1)}, u32[]{:S(2)}, u32[]{:S(2)}) async-start(bf16[4,3,1024,64]{2,3,1,0:T(8,128)(2,1)} %pad_maximum_fusion.1), calls=%async_computation.2 | async-start | bytes 3145728 | tf_op jit(solution)/shard_map/all_to_all | solution.py:231
  541.3 43.2 %all-to-all-start = ((bf16[4,3,1024,64]{2,3,1,0:T(8,128)(2,1)}), bf16[4,3,1024,64]{2,3,1,0:T(8,128)(2,1)}, u32[]{:S(2)}, u32[]{:S(2)}) async-start(bf16[4,3,1024,64]{2,3,1,0:T(8,128)(2,1)} %pad_maximum_fusion), calls=%async_computation.1 | async-start | bytes 3145728 | tf_op jit(solution)/shard_map/all_to_all | solution.py:230
  549.2 191.3 %copy-start.1 = (bf16[64,4608]{1,0:T(8,128)(2,1)S(1)}, bf16[64,4608]{1,0:T(8,128)(2,1)}, u32[]{:S(2)}) copy-start(bf16[64,4608]{1,0:T(8,128)(2,1)} %param.16) | copy-start | bytes 1769476
  549.2 191.3 %copy-start.4 = (f32[4608]{0:T(1024)S(1)}, f32[4608]{0:T(1024)}, u32[]{:S(2)}) copy-start(f32[4608]{0:T(1024)} %param.22) | copy-start | bytes 55300
Sparse Core Ops, SparseCore 0:
  10.9 214.5 all-gather.3
  248.1 20.9 all-gather.5
  270.8 26.0 all-gather.7
  488.3 250.9 reduce-scatter.1
where the time goes:
time: 754 us; the launch traced here: 749 us
  waiting for transfers between devices  473 us (63%)
  loops' own time  80.9 us (11%)
  matrix products  59.2 us (8%)
  local copies, waits for them, and re-layouts  56.5 us (7%)
  other arithmetic  40 us (5%)
  between operations  26.2 us (3%)
  starting transfers between devices  13.6 us (2%)
    all_gather x1, waiting for transfers between devices, on_device(): lax.all_gather(normed, 'tensor', axis=0, tiled=True)  207 us
    reduce_scatter x1, waiting for transfers between devices, on_device(): lax.psum_scatter(jnp.dot(attn_rows, out_weight, preferred_element_type=jn...  153 us
    another operation x1, loops' own time, on_device(): numer, denom = lax.fori_loop(0, row_count // width, tile, start_state)  80.2 us
    all_to_all x1, waiting for transfers between devices, on_device(): lax.all_to_all(send_keys, 'seq', split_axis=0, concat_axis=0, tiled=True)  34.4 us
    all_to_all x1, waiting for transfers between devices, on_device(): lax.all_to_all(send_values, 'seq', split_axis=0, concat_axis=0, tiled=True)  32 us
    dot_general x16, matrix products, compute(): jnp.einsum('qcgd,kcd->cgqk', my_queries[which_half], k_block, preferred_e...  30.9 us
    all_gather x1, waiting for transfers between devices, on_device(): value_rows = lax.all_gather(v_rot, 'seq', axis=0, tiled=True)  27.7 us
    dynamic_slice x32, local copies, waits for them, and re-layouts, tile(): v_block = lax.dynamic_slice_in_dim(value_rows, tile_index * width, width, 0)  17.8 us
  transfers between devices with their start and end apart: 8, of which 8 were waited for; matrix products, arithmetic and copies ran while one was open for 3% of the time, Pallas kernels for 0%

commit v1 on v0

v1 whole, which is shorter than its diff:
```python
import jax
import jax.numpy as jnp
import numpy as np
from jax import lax
from jax.sharding import Mesh
from jax.sharding import PartitionSpec as P

HD = 128


EPSILON = 1e-06
SOFTCAP = 50.0
QUERY_SCALE = 144.0 ** (-0.5)
SCORE_SHIFT = 20.0
ROPE_BASE = 10000.0
KEY_TILE = 512
Q_CHUNKS = 2


def rms_scale(values, gain):
    mean_sq = jnp.mean(values * values, axis=-1, keepdims=True)
    return values * lax.rsqrt(mean_sq + EPSILON) * gain


def rotate(values, positions):
    head_dim = values.shape[-1]
    half_dim = head_dim // 2
    freqs = ROPE_BASE ** (-2.0 * jnp.arange(half_dim, dtype=jnp.float32) / head_dim)
    angles = positions.astype(jnp.float32)[:, None] * freqs[None, :]
    cosine = jnp.cos(angles)[:, None, :]
    sine = jnp.sin(angles)[:, None, :]
    first = values[..., :half_dim]
    second = values[..., half_dim:]
    return jnp.concatenate(
        [first * cosine - second * sine, second * cosine + first * sine], axis=-1
    )


def segment_starts_of(row_segments, seg_lengths):
    starts = jnp.cumsum(seg_lengths) - seg_lengths
    request_ids = jnp.arange(seg_lengths.shape[0], dtype=jnp.int32)
    return jnp.sum(
        jnp.where(row_segments[:, None] == request_ids[None, :], starts[None, :], 0), axis=1
    )


def swap(value, axis):
    return lax.ppermute(value, axis, [(0, 1), (1, 0)])


def on_device(
    hidden_in,
    norm_gain,
    query_weight,
    key_weight,
    value_weight,
    out_weight,
    post_gain,
    seg_lengths,
    segment_ids,
    slot_map,
):
    n_group = lax.axis_size("th")
    n_seq = lax.axis_size("seq")
    n_pair = lax.axis_size("tl")
    local_rows = hidden_in.shape[0]
    tokens = segment_ids.shape[0]
    group_rows = local_rows * n_group
    seq_rows = group_rows * n_pair
    head_dim = HD
    half_kv = key_weight.shape[1]
    seq_index = lax.axis_index("seq")
    pair_index = lax.axis_index("tl")
    slot_count = seg_lengths.shape[0]

    hidden = hidden_in.astype(jnp.float32)
    normed = rms_scale(hidden, norm_gain).astype(jnp.bfloat16)

    own_joined = jnp.concatenate([query_weight, key_weight, value_weight], axis=1)
    other_joined = swap(own_joined, "tl")
    other_out = swap(out_weight, "tl")

    spread = jnp.broadcast_to(normed[None], (n_group,) + normed.shape)
    gathered = lax.all_to_all(spread, "th", 0, 0, tiled=True).reshape(group_rows, -1)
    mixed = jnp.dot(
        gathered,
        jnp.concatenate([own_joined, other_joined], axis=1),
        preferred_element_type=jnp.float32,
    )
    width = own_joined.shape[1]
    q_own = mixed[:, :head_dim]
    k_own = mixed[:, head_dim : head_dim + half_kv]
    v_own = mixed[:, head_dim + half_kv : width]
    q_other = mixed[:, width : width + head_dim]
    k_other = mixed[:, width + head_dim : width + head_dim + half_kv]
    v_other = mixed[:, width + head_dim + half_kv :]
    leading = pair_index == 0
    full_key = jnp.where(
        leading, jnp.concatenate([k_own, k_other], 1), jnp.concatenate([k_other, k_own], 1)
    )
    full_value = jnp.where(
        leading, jnp.concatenate([v_own, v_other], 1), jnp.concatenate([v_other, v_own], 1)
    )

    member = jnp.arange(group_rows, dtype=jnp.int32) // local_rows
    within = jnp.arange(group_rows, dtype=jnp.int32) % local_rows
    row_ids = seq_index * seq_rows + (member * n_pair + pair_index) * local_rows + within
    row_segments = jnp.take(segment_ids, row_ids)
    positions = row_ids - segment_starts_of(row_segments, seg_lengths)

    q_rot = rotate(jnp.stack([q_own, q_other], axis=1), positions).astype(jnp.bfloat16)
    k_rot = rotate(full_key[:, None, :], positions)[:, 0].astype(jnp.bfloat16)
    v_bf = full_value.astype(jnp.bfloat16)

    kv = jnp.concatenate([k_rot, v_bf], axis=1)
    kv_all = lax.all_gather(kv, ("seq", "tl"), axis=0, tiled=True)
    kv_all = kv_all.reshape(n_seq, n_pair, n_group, local_rows, 2 * head_dim)
    kv_all = jnp.transpose(kv_all, (0, 2, 1, 3, 4)).reshape(tokens, 2 * head_dim)
    key_rows = kv_all[:, :head_dim]
    value_rows = kv_all[:, head_dim:]

    chunk_rows = group_rows // Q_CHUNKS
    q_chunks = q_rot.reshape(Q_CHUNKS, chunk_rows, 2, head_dim)
    q_ids = row_ids.reshape(Q_CHUNKS, chunk_rows)
    q_segs = row_segments.reshape(Q_CHUNKS, chunk_rows)
    zero_numer = jnp.zeros((chunk_rows, 2, head_dim), jnp.float32)
    zero_denom = jnp.zeros((2, chunk_rows), jnp.float32)
    start_state = (
        tuple(zero_numer for _ in range(Q_CHUNKS)),
        tuple(zero_denom for _ in range(Q_CHUNKS)),
    )
    first_needed = jnp.min(row_ids - positions)
    lo_tile = first_needed // KEY_TILE
    hi_tile = (jnp.max(row_ids) // KEY_TILE) + 1

    def tile(tile_index, state):
        numer, denom = state
        k_start = tile_index * KEY_TILE
        k_block = lax.dynamic_slice_in_dim(key_rows, k_start, KEY_TILE, 0)
        v_block = lax.dynamic_slice_in_dim(value_rows, k_start, KEY_TILE, 0)
        k_segs = lax.dynamic_slice_in_dim(segment_ids, k_start, KEY_TILE, 0)
        k_ids = k_start + jnp.arange(KEY_TILE, dtype=jnp.int32)
        new_numer = []
        new_denom = []
        for chunk in range(Q_CHUNKS):

            def compute(pair, chunk=chunk):
                numer_one, denom_one = pair
                scores = (
                    jnp.einsum(
                        "qhd,kd->hqk",
                        q_chunks[chunk],
                        k_block,
                        preferred_element_type=jnp.float32,
                    )
                    * QUERY_SCALE
                )
                scores = SOFTCAP * jnp.tanh(scores / SOFTCAP)
                live = (k_ids[None, :] <= q_ids[chunk][:, None]) & (
                    k_segs[None, :] == q_segs[chunk][:, None]
                )
                weights = jnp.where(live[None], jnp.exp(scores - SCORE_SHIFT), 0.0)
                denom_one = denom_one + jnp.sum(weights, axis=-1)
                numer_one = numer_one + jnp.einsum(
                    "hqk,kd->qhd",
                    weights.astype(jnp.bfloat16),
                    v_block,
                    preferred_element_type=jnp.float32,
                )
                return (numer_one, denom_one)

            useful = (
                (k_start <= q_ids[chunk][-1])
                & (k_segs[0] <= q_segs[chunk][-1])
                & (k_segs[-1] >= q_segs[chunk][0])
            )
            numer_one, denom_one = lax.cond(
                useful, compute, lambda pair: pair, (numer[chunk], denom[chunk])
            )
            new_numer.append(numer_one)
            new_denom.append(denom_one)
        return (tuple(new_numer), tuple(new_denom))

    numer, denom = lax.fori_loop(lo_tile, hi_tile, tile, start_state)
    finished = []
    for chunk in range(Q_CHUNKS):
        denom_rows = jnp.transpose(denom[chunk], (1, 0))[..., None]
        finished.append((numer[chunk] / denom_rows).astype(jnp.bfloat16))
    attended = jnp.concatenate(finished, axis=0).reshape(group_rows, 2 * head_dim)
    partial = jnp.dot(
        attended,
        jnp.concatenate([out_weight, other_out], axis=0),
        preferred_element_type=jnp.float32,
    ).astype(jnp.bfloat16)
    pieces = lax.all_to_all(
        partial.reshape(n_group, local_rows, -1), "th", 0, 0, tiled=True
    )
    projected = jnp.sum(pieces.astype(jnp.float32), axis=0)
    hidden_out = (hidden + rms_scale(projected, post_gain)).astype(jnp.bfloat16)

    cache_len = tokens // 2
    part_len = cache_len // n_seq
    request_ids = jnp.arange(slot_count, dtype=jnp.int32)
    starts = jnp.cumsum(seg_lengths) - seg_lengths
    own_offset = pair_index * half_kv
    own_keys = lax.dynamic_slice_in_dim(key_rows, own_offset, half_kv, 1)
    own_values = lax.dynamic_slice_in_dim(value_rows, own_offset, half_kv, 1)
    keys_pad = jnp.concatenate([own_keys, jnp.zeros((cache_len, half_kv), jnp.bfloat16)], 0)
    values_pad = jnp.concatenate(
        [own_values, jnp.zeros((cache_len, half_kv), jnp.bfloat16)], 0
    )
    seg_pad = jnp.concatenate([segment_ids, jnp.full((cache_len,), -1, jnp.int32)], 0)
    key_slots = []
    value_slots = []
    for slot_index in range(slot_count):
        request = jnp.sum(jnp.where(slot_map == slot_index, request_ids, 0)).astype(jnp.int32)
        first_row = jnp.sum(jnp.where(request_ids == request, starts, 0)).astype(jnp.int32)
        row0 = first_row + seq_index * part_len
        keep = (lax.dynamic_slice_in_dim(seg_pad, row0, part_len, 0) == request)[:, None]
        key_slots.append(
            jnp.where(
                keep,
                lax.dynamic_slice_in_dim(keys_pad, row0, part_len, 0),
                jnp.zeros((), jnp.bfloat16),
            )
        )
        value_slots.append(
            jnp.where(
                keep,
                lax.dynamic_slice_in_dim(values_pad, row0, part_len, 0),
                jnp.zeros((), jnp.bfloat16),
            )
        )
    return (hidden_out, jnp.stack(key_slots), jnp.stack(value_slots))


def solution(mesh):
    devices = np.asarray(mesh.devices)
    n_seq, n_tensor = devices.shape
    split = Mesh(devices.reshape(n_seq, n_tensor // 2, 2), ("seq", "th", "tl"))
    rows = P(("seq", "th", "tl"), None)
    cols = P(None, ("th", "tl"))
    return jax.shard_map(
        on_device,
        mesh=split,
        in_specs=(
            rows,
            P(),
            cols,
            cols,
            cols,
            P(("th", "tl"), None),
            P(),
            P(),
            P(),
            P(),
        ),
        out_specs=(rows, P(None, "seq", ("th", "tl")), P(None, "seq", ("th", "tl"))),
        check_vma=False,
    )
```

time: 754 us -> 502 us (0.67)
  the two profiles are of different devices: /device:TPU:4 before, /device:TPU:7 now
where the time goes in v1:
time: 502 us; the launch traced here: 503 us
  waiting for transfers between devices  262 us (52%)
  loops' own time  69.8 us (14%)
  local copies, waits for them, and re-layouts  56.3 us (11%)
  matrix products  45.3 us (9%)
  other arithmetic  30.3 us (6%)
  between operations  21.1 us (4%)
  starting transfers between devices  18.2 us (4%)
    ppermute x2, waiting for transfers between devices, swap(): return lax.ppermute(value, axis, [(0, 1), (1, 0)])  136 us
    all_to_all x1, waiting for transfers between devices, on_device(): lax.all_to_all(partial.reshape(n_group, local_rows, -1), 'th', 0, 0, tile...  86.6 us
    another operation x1, loops' own time, on_device(): numer, denom = lax.fori_loop(lo_tile, hi_tile, tile, start_state)  69 us
    all_gather x1, waiting for transfers between devices, on_device(): kv_all = lax.all_gather(kv, ('seq', 'tl'), axis=0, tiled=True)  39 us
    dot_general x12, matrix products, compute(): jnp.einsum('qhd,kd->hqk', q_chunks[chunk], k_block, preferred_element_typ...  22.5 us
    dynamic_slice x11, local copies, waits for them, and re-layouts, tile(): v_block = lax.dynamic_slice_in_dim(value_rows, k_start, KEY_TILE, 0)  10.2 us
  transfers between devices with their start and end apart: 5, of which 3 were waited for; matrix products, arithmetic and copies ran while one was open for 20% of the time, Pallas kernels for 0%

profile of v1, /device:TPU:7, one launch (start us, length us, event | category | flops | bytes accessed | tf_op | source)
XLA Modules:
  0.0 502.7 jit_solution(8622895595097249006)
XLA Ops:
  9.7 4.6 broadcast_in_dim.129
  14.3 8.8 %all-to-all-start = ((bf16[16,64,4608]{2,1,0:T(8,128)(2,1)}), bf16[16,64,4608]{2,1,0:T(8,128)(2,1)}, u32[]{:S(2)}, u32[]{:S(2)}) async-start(bf16[16,64,4608]{2,1,0:T(8,128)(2,1)} %broadcast_in_dim.129), calls=%async_computation | async-start | bytes 18874368 | tf_op jit(solution)/shard_map/all_to_all | solution.py:84
  25.0 3.5 pad_maximum_fusion
  29.4 6.2 %gather_fusion = s32[1024]{0:T(1024)S(1)} fusion(s32[8192]{0:T(1024)S(1)} %copy-done, s32[1024]{0:T(1024)S(1)} %broadcast_clamp_fusion), kind=kCustom, calls=%fused_computation | custom fusion | bytes 12288 | tf_op jit(solution)/shard_map/jit(_take)/gather | solution.py:108
  39.6 136.1 %collective-permute-done = bf16[4608,256]{1,0:T(8,128)(2,1)} collective-permute-done((bf16[4608,256]{1,0:T(8,128)(2,1)}, bf16[4608,256]{1,0:T(8,128)(2,1)}, u32[]{:S(2)}, u32[]{:S(2)}) %collective-permute-start) | collective-permute-done | bytes 2359328 | tf_op jit(solution)/shard_map/ppermute | solution.py:48
  175.7 9.7 %fusion.12 = f32[1024,512]{0,1:T(8,128)S(1)} fusion(bf16[1024,4608]{1,0:T(8,128)(2,1)} %bitcast.25, bf16[4608,256]{1,0:T(8,128)(2,1)} %collective-permute-done, bf16[4608,64]{1,0:T(8,128)(2,1)S(1)} %copy.43, bf16[4608,64]{1,0:T(8,128)(2,1)S(1)} %copy.42, bf16[4608,128]{1,0:T(8,128)(2,1)} %param.18), kind=kOutput, calls=%fused_computation.24 | convolution fusion | flops 4850712576 | bytes 16252928 | tf_op jit(solution)/shard_map/dot_general | solution.py:85
  198.1 39.0 %all-gather.2.cloned.1.call-done = bf16[8192,256]{0,1:T(8,128)(2,1)} async-done(((bf16[1024,256]{0,1:T(8,128)(2,1)}), bf16[8192,256]{0,1:T(8,128)(2,1)}) %all-gather.2.cloned.1.call-update) | async-done | bytes 4194320 | tf_op jit(solution)/shard_map/all_gather | solution.py:116
  237.1 6.4 %copy.44 = bf16[8192,256]{1,0:T(8,128)(2,1)} copy(bf16[8192,256]{0,1:T(8,128)(2,1)} %all-gather.2.cloned.1.call-done) | data formatting | bytes 8388608 | tf_op jit(solution)/shard_map/all_gather | solution.py:116
  247.6 127.1 %while.16 = (s32[]{:T(128)}, f32[512,2,128]{2,0,1:T(8,128)S(1)}, f32[512,2,128]{2,0,1:T(8,128)S(1)}, f32[2,512]{1,0:T(2,128)S(1)}, f32[2,512]{1,0:T(2,128)S(1)},...) while((s32[]{:T(128)}, f32[512,2,128]{2,0,1:T(8,128)S(1)}, ...), condition=%wide.region_12.13_spmd, body=%wide.region_5.12_spmd.sunk | while | flops 544997888 | bytes 8985155 | solution.py:184
  253.0 2.7 conditional.4
  264.3 2.8 conditional.4
  275.6 2.8 conditional.4
  286.9 2.8 conditional.4
  298.2 2.8 conditional.4
  309.5 2.8 conditional.4
  320.8 2.8 conditional.4
  332.1 2.8 conditional.4
  343.4 2.8 conditional.4
  349.3 2.7 conditional.5
  371.9 2.7 conditional.5
  377.1 6.7 %convolution_convert_fusion = bf16[1024,4608]{1,0:T(8,128)(2,1)} fusion(bf16[1024,256]{0,1:T(8,128)(2,1)S(1)} %bitcast.113, bf16[128,4608]{1,0:T(8,128)(2,1)} %collective-permute-done.1, bf16[128,4608]{1,0:T(8,128)(2,1)} %param.21), kind=kOutput, calls=%fused_computation.23 | convolution fusion | flops 2425356288 | bytes 12320768 | tf_op jit(solution)/shard_map/dot_general | solution.py:190
  383.8 7.6 %all-to-all-start.1 = ((bf16[16,64,4608]{2,1,0:T(8,128)(2,1)}), bf16[16,64,4608]{2,1,0:T(8,128)(2,1)}, u32[]{:S(2)}, u32[]{:S(2)}) async-start(bf16[16,64,4608]{2,1,0:T(8,128)(2,1)} %bitcast.110), calls=%async_computation.1 | async-start | bytes 18874368 | tf_op jit(solution)/shard_map/all_to_all | solution.py:195
  402.8 86.6 %all-to-all-done.1 = bf16[16,64,4608]{2,1,0:T(8,128)(2,1)} async-done(((bf16[16,64,4608]{2,1,0:T(8,128)(2,1)}), bf16[16,64,4608]{2,1,0:T(8,128)(2,1)}, u32[]{:S(2)}, u32[]{:S(2)}) %all-to-all-start.1) | async-done | bytes 9437216 | tf_op jit(solution)/shard_map/all_to_all | solution.py:195
  489.5 5.1 %convert_reduce_fusion = f32[64,4608]{1,0:T(8,128)S(1)} fusion(bf16[16,64,4608]{2,1,0:T(8,128)(2,1)} %all-to-all-done.1), kind=kLoop, calls=%fused_computation.22 | loop fusion | flops 9142272 | bytes 10616832 | tf_op jit(solution)/shard_map/reduce_sum | solution.py:198
  (213 shorter events, 94.4 us)
Async XLA Ops:
  14.3 8.9 %copy-start.3 = (bf16[4608,64]{0,1:T(8,128)(2,1)S(1)}, bf16[4608,64]{0,1:T(8,128)(2,1)}, u32[]{:S(2)}) copy-start(bf16[4608,64]{0,1:T(8,128)(2,1)} %param.20) | copy-start | bytes 1769476
  14.3 161.4 %all-to-all-start = ((bf16[16,64,4608]{2,1,0:T(8,128)(2,1)}), bf16[16,64,4608]{2,1,0:T(8,128)(2,1)}, u32[]{:S(2)}, u32[]{:S(2)}) async-start(bf16[16,64,4608]{2,1,0:T(8,128)(2,1)} %broadcast_in_dim.129), calls=%async_computation | async-start | bytes 18874368 | tf_op jit(solution)/shard_map/all_to_all | solution.py:84
  23.1 1.1 copy-start.4
  23.1 213.9 %all-gather.2.cloned.1.call-start = ((), (), s32[]{:S(2)}) async-start(), calls=%async_computation.2 | async-start | bytes 4718592 | tf_op jit(solution)/shard_map/all_gather | solution.py:116
  24.9 4.2 copy-start.6
  24.9 4.4 copy-start
  28.4 147.3 %collective-permute-start = (bf16[4608,256]{1,0:T(8,128)(2,1)}, bf16[4608,256]{1,0:T(8,128)(2,1)}, u32[]{:S(2)}, u32[]{:S(2)}) collective-permute-start(bf16[4608,256]{1,0:T(8,128)(2,1)} %pad_maximum_fusion), channel_id=1, source_target_pairs={{0,1},{1,0},{2,3},{3,2},{4,5},{5,4},{6,7},{7,6},{8,9},{9,8},{10,11... | collective-permute-start | bytes 7077896 | tf_op jit(solution)/shard_map/ppermute | solution.py:48
  29.4 6.2 %copy-start.7 = (s32[3]{0:T(128)S(1)}, s32[3]{0:T(128)}, u32[]{:S(2)}) copy-start(s32[3]{0:T(128)} %param.25) | copy-start | bytes 40
  185.5 1.4 copy-start.2
  187.7 189.4 %collective-permute-start.1 = (bf16[128,4608]{1,0:T(8,128)(2,1)}, bf16[128,4608]{1,0:T(8,128)(2,1)}, u32[]{:S(2)}, u32[]{:S(2)}) collective-permute-start(bf16[128,4608]{1,0:T(8,128)(2,1)} %param.21), channel_id=1, source_target_pairs={{0,1},{1,0},{2,3},{3,2},{4,5},{5,4},{6,7},{7,6},{8,9},{9,8},{10,11... | collective-permute-start | bytes 3538952 | tf_op jit(solution)/shard_map/ppermute | solution.py:48
  383.8 105.7 %all-to-all-start.1 = ((bf16[16,64,4608]{2,1,0:T(8,128)(2,1)}), bf16[16,64,4608]{2,1,0:T(8,128)(2,1)}, u32[]{:S(2)}, u32[]{:S(2)}) async-start(bf16[16,64,4608]{2,1,0:T(8,128)(2,1)} %bitcast.110), calls=%async_computation.1 | async-start | bytes 18874368 | tf_op jit(solution)/shard_map/all_to_all | solution.py:195
  402.8 92.0 %copy-start.1 = (bf16[64,4608]{1,0:T(8,128)(2,1)S(1)}, bf16[64,4608]{1,0:T(8,128)(2,1)}, u32[]{:S(2)}) copy-start(bf16[64,4608]{1,0:T(8,128)(2,1)} %param.16) | copy-start | bytes 1769476
  402.8 92.0 %copy-start.5 = (f32[4608]{0:T(1024)S(1)}, f32[4608]{0:T(1024)}, u32[]{:S(2)}) copy-start(f32[4608]{0:T(1024)} %param.22) | copy-start | bytes 55300
Sparse Core Ops, SparseCore 0:
  187.8 49.1 all-gather.1
